TPU v7x, 256 devices: a whole 4x4x8 slice. The times are simulated.
256 devices in a mesh: dp: 32 (over x, z), tensor: 8 (over y, core).
Axes of the slice: x: 4, y: 4, z: 8, core: 2. Of those that a mesh axis runs over, the one named last changes fastest.
Arguments:
- counts: int32 [32], replicated, may hold values from 1 to 32, 512 in all
- keys: bfloat16 [1024, 28672], P('dp'), may hold values from -6 to 6
- inverse_cov: bfloat16 [28672, 28672], P('tensor', 'dp'), as said below
- hidden: bfloat16 [1024, 8192], P('dp', 'tensor'), may hold values from -6 to 6
- targets: bfloat16 [1024, 8192], P('dp', 'tensor'), may hold values from -48 to 48
- down_weight: bfloat16 [8192, 28672], P('tensor', 'dp'), may hold values from -0.03125 to 0.03125
Outputs:
- new_weight: bfloat16 [8192, 28672], P('tensor', 'dp')
- next_resid: bfloat16 [1024, 8192], P('dp', 'tensor')
Inputs may be any that keep to these rules, and one draw needn't show every extreme that they name: Group g has counts[g] live edits in its first counts[g] slots; the counts sum to 512; some group holds 32. `inverse_cov`: symmetric positive definite.
All inputs are finite; a program needn't handle non-finite values.
Results may differ from a plain program's by a relative error of at most 0.01.
The roundings to bfloat16 on the way count: a program that leaves them out, or rounds other values in their place, can miss the bound.
Values may be sent and summed in bfloat16 or wider, within the bound.
No kernel may reach another device: no remote copies, remote signals or barrier semaphores. Data moves between devices by JAX's collectives and lax.ppermute only.
A program may use at most 128 MiB of HBM per device.

v0:
```python
import jax
import jax.numpy as jnp
from jax import lax
from jax.sharding import PartitionSpec as P

LAYERS_LEFT = 3


def cholesky_solve(system, right_side):
    factor = jnp.linalg.cholesky(system)
    middle = lax.linalg.triangular_solve(factor, right_side, left_side=True, lower=True)
    return lax.linalg.triangular_solve(factor, middle, left_side=True, lower=True, transpose_a=True)


def rows_product(left, right):
    return lax.dot_general(
        left, right, (((1,), (1,)), ((), ())), preferred_element_type=jnp.float32
    )


def pick(select, values):
    return jnp.dot(select, values, preferred_element_type=jnp.float32).astype(values.dtype)


def gather_rows(x, axis):
    n = lax.axis_size(axis)
    copies = jnp.broadcast_to(x[None], (n,) + x.shape)
    return lax.all_to_all(copies, axis, 0, 0, tiled=True).reshape((n * x.shape[0],) + x.shape[1:])


def scatter_rows_sum(x, axis):
    n = lax.axis_size(axis)
    parts = lax.all_to_all(x.reshape((n, x.shape[0] // n) + x.shape[1:]), axis, 0, 0, tiled=True)
    return parts.sum(0)


def per_device(counts, keys, inverse_cov, hidden, targets, down_weight):
    slot_count = keys.shape[0]
    group_size = lax.axis_size("dp")
    group_index = lax.axis_index("dp")
    tensor_index = lax.axis_index("tensor")
    width_part = inverse_cov.shape[0]
    row_total = slot_count * group_size
    live_total = row_total // 2
    ends = jnp.cumsum(counts)
    starts = ends - counts
    compact = jnp.arange(live_total, dtype=jnp.int32)
    owner = jnp.minimum(jnp.sum(compact[:, None] >= ends[None, :], axis=1), group_size - 1)
    row_of = owner * slot_count + compact - starts[owner]
    select = (row_of[:, None] == jnp.arange(row_total, dtype=jnp.int32)[None, :]).astype(
        jnp.bfloat16
    )
    slots = jnp.arange(slot_count, dtype=jnp.int32)
    live_vec = slots < counts[group_index]
    live_slot = live_vec[:, None]
    own_compact = jnp.where(live_vec, starts[group_index] + slots, 0)
    masked_keys = jnp.where(live_slot, keys, jnp.zeros_like(keys))
    column_part = lax.dynamic_slice_in_dim(masked_keys, tensor_index * width_part, width_part, 1)
    columns = lax.all_to_all(masked_keys, "dp", split_axis=1, concat_axis=0, tiled=True)
    gathered = lax.all_gather(column_part, "dp", axis=0, tiled=True)
    change = (targets.astype(jnp.float32) - hidden.astype(jnp.float32)) / LAYERS_LEFT
    resid_local = jnp.where(live_slot, change, jnp.zeros_like(change)).astype(jnp.bfloat16)
    gathered, columns = lax.optimization_barrier((gathered, columns))
    resid_all = lax.all_gather(resid_local, "dp", axis=0, tiled=True)
    keys_c = pick(select, gathered)
    columns_c = pick(select, columns)
    partial_q = jnp.dot(keys_c, inverse_cov, preferred_element_type=jnp.float32)
    tensor_size = lax.axis_size("tensor")
    parts_q = (
        lax.all_to_all(
            partial_q.astype(jnp.bfloat16).reshape((tensor_size, -1) + partial_q.shape[1:]),
            "tensor",
            0,
            0,
            tiled=True,
        )
        .astype(jnp.float32)
        .sum(0)
    )
    precond_c = gather_rows(parts_q.astype(jnp.bfloat16), "tensor")
    gram_c = gather_rows(scatter_rows_sum(rows_product(precond_c, columns_c), "dp"), "dp")
    base_partial = rows_product(columns, down_weight)
    gram_c, base_partial = lax.optimization_barrier((gram_c, base_partial))
    base = scatter_rows_sum(base_partial, "dp")
    system = gram_c + jnp.eye(live_total, dtype=jnp.float32)
    factor = jnp.linalg.cholesky(system)
    factor, resid_all = lax.optimization_barrier((factor, resid_all))
    resid_c = pick(select, resid_all)
    middle = lax.linalg.triangular_solve(
        factor, resid_c.astype(jnp.float32), left_side=True, lower=True
    )
    solved_c = lax.linalg.triangular_solve(
        factor, middle, left_side=True, lower=True, transpose_a=True
    ).astype(jnp.bfloat16)
    weight_delta = lax.dot_general(
        solved_c, precond_c, (((0,), (0,)), ((), ())), preferred_element_type=jnp.float32
    )
    new_weight = (down_weight.astype(jnp.float32) + weight_delta).astype(jnp.bfloat16)
    gram_own = jnp.where(live_slot, jnp.take(gram_c, own_compact, axis=1).T, 0.0)
    extra = jnp.dot(
        gram_own,
        solved_c.astype(jnp.float32),
        precision=lax.Precision.HIGHEST,
        preferred_element_type=jnp.float32,
    )
    summed = hidden.astype(jnp.float32) + (base + extra)
    next_resid = jnp.where(live_slot, summed, jnp.zeros_like(summed)).astype(jnp.bfloat16)
    return (new_weight, next_resid)


def solution(mesh):
    in_specs = (
        P(),
        P("dp", None),
        P("tensor", "dp"),
        P("dp", "tensor"),
        P("dp", "tensor"),
        P("tensor", "dp"),
    )
    out_specs = (P("tensor", "dp"), P("dp", "tensor"))
    return jax.shard_map(
        per_device, mesh=mesh, in_specs=in_specs, out_specs=out_specs, check_vma=False
    )
```

profile of v0, /device:TPU:2, one launch (start us, length us, event | category | flops | bytes accessed | tf_op | source)
XLA Modules:
  0.0 408.6 jit_solution(1317642860902086746)
XLA Ops:
  12.9 11.7 %all-to-all-start = ((bf16[32,32,896]{2,0,1:T(8,128)(2,1)}), bf16[32,32,896]{2,0,1:T(8,128)(2,1)S(1)}, u32[]{:S(2)}, u32[]{:S(2)}) async-start(bf16[32,32,896]{2,0,1:T(8,128)(2,1)} %bitcast.127), calls=%async_computation | async-start | bytes 3670016 | tf_op jit(solution)/shard_map/all_to_all | solution.py:59
  26.4 4.4 %compare_select_fusion.1 = (s32[512,1]{0,1:T(1,128)S(1)}, s32[512,1]{0,1:T(1,128)S(1)}) fusion(s32[]{:T(128)} %bitcast.27, s32[]{:T(128)} %bitcast.28, s32[]{:T(128)} %bitcast.29, s32[]{:T(128)} %bitcast.30, s32[]{:T(128)} %bitcast.31, s32[]{:T(128)} %bitcast.33, s32[]{:T(128)} %bitcast.32, s32[512,1]{0,1:T(1,128)S(1)} %bitcast.136), kind=kLoop, calls=%fused_computation.136 | loop fusion | flops 7680 | bytes 6172 | tf_op jit(solution)/shard_map/gather | solution.py:49
  31.0 15.8 %select_subtract_fusion = s32[512]{0:T(512)S(1)} fusion(pred[512]{0:T(512)(128)(4,1)S(1)} %get-tuple-element.46, pred[512]{0:T(512)(128)(4,1)S(1)} %get-tuple-element.45, pred[512]{0:T(512)(128)(4,1)S(1)} %get-tuple-element.44, pred[512]{0:T(512)(128)(4,1)S(1)} %get-tuple-element.43, pred[512]{0:T(512)(128)(4,1)S(1)} %get-tuple-element.42, ...), kind=kLoop, calls=%fused_computation.145 | loop fusion | flops 14848 | bytes 19044 | tf_op jit(solution)/shard_map/sub | solution.py:49
  46.8 28.5 %all-to-all-done = bf16[32,32,896]{2,0,1:T(8,128)(2,1)S(1)} async-done(((bf16[32,32,896]{2,0,1:T(8,128)(2,1)}), bf16[32,32,896]{2,0,1:T(8,128)(2,1)S(1)}, u32[]{:S(2)}, u32[]{:S(2)}) %all-to-all-start) | async-done | bytes 1835040 | tf_op jit(solution)/shard_map/all_to_all | solution.py:59
  75.4 41.5 %all-gather.3.cloned.1.call-done = bf16[1024,3584]{1,0:T(8,128)(2,1)} async-done(((bf16[32,3584]{1,0:T(8,128)(2,1)}), bf16[1024,3584]{1,0:T(8,128)(2,1)}) %all-gather.3.cloned.1.call-update) | async-done | bytes 7340048 | tf_op jit(solution)/shard_map/all_gather | solution.py:60
  116.9 13.7 %convolution_convert_fusion.1 = bf16[512,896]{1,0:T(8,128)(2,1)} fusion(bf16[3584,896]{1,0:T(8,128)(2,1)} %param.8, bf16[1024,3584]{1,0:T(8,128)(2,1)} %all-gather.3.cloned.1.call-done, s32[512]{0:T(512)S(1)} %select_subtract_fusion), kind=kOutput, calls=%fused_computation.24 | convolution fusion | flops 7049248768 | bytes 14682112 | tf_op jit(solution)/shard_map/dot_general | solution.py:67
  130.5 18.9 %all_to_all.44 = bf16[8,64,896]{2,1,0:T(8,128)(2,1)S(1)} all-to-all(bf16[8,64,896]{2,1,0:T(8,128)(2,1)} %bitcast.134), channel_id=1, replica_groups=mesh['dp'=32,'tensor'=8] {'tensor'}, dimensions={0} | all-to-all | bytes 1835008 | tf_op jit(solution)/shard_map/all_to_all | solution.py:70
  149.6 17.7 %all_to_all.45 = bf16[8,64,896]{2,1,0:T(8,128)(2,1)} all-to-all(bf16[8,64,896]{2,1,0:T(8,128)(2,1)S(1)} %broadcast_in_dim.72), channel_id=1, replica_groups=mesh['dp'=32,'tensor'=8] {'tensor'}, dimensions={0} | all-to-all | bytes 1835008 | tf_op jit(solution)/shard_map/all_to_all | solution.py:28
  167.3 3.0 fusion.37
  170.3 33.0 %all_to_all.46 = f32[32,16,512]{2,1,0:T(8,128)S(1)} all-to-all(f32[32,16,512]{2,1,0:T(8,128)S(1)} %fusion.37), channel_id=1, replica_groups=mesh['dp'=32,'tensor'=8] {'dp'}, dimensions={0} | all-to-all | bytes 2097152 | tf_op jit(solution)/shard_map/all_to_all | solution.py:33
  204.5 7.5 %all-to-all-start.4 = ((f32[32,16,512]{2,1,0:T(8,128)}), f32[32,16,512]{2,1,0:T(8,128)S(1)}, u32[]{:S(2)}, u32[]{:S(2)}) async-start(f32[32,16,512]{2,1,0:T(8,128)} %broadcast_in_dim.73), calls=%async_computation.4 | async-start | bytes 2097152 | tf_op jit(solution)/shard_map/all_to_all | solution.py:28
  216.7 6.3 %fusion.88 = f32[1024,1024]{1,0:T(8,128)} fusion(bf16[1024,896]{1,0:T(8,128)(2,1)} %bitcast.131, bf16[1024,896]{1,0:T(8,128)(2,1)} %param.11), kind=kOutput, calls=%fused_computation.176 | convolution fusion | flops 1879048192 | bytes 7864320 | tf_op jit(solution)/shard_map/dot_general | solution.py:16
  223.0 15.5 %all-to-all-done.4 = f32[32,16,512]{2,1,0:T(8,128)S(1)} async-done(((f32[32,16,512]{2,1,0:T(8,128)}), f32[32,16,512]{2,1,0:T(8,128)S(1)}, u32[]{:S(2)}, u32[]{:S(2)}) %all-to-all-start.4) | async-done | bytes 1048608 | tf_op jit(solution)/shard_map/all_to_all | solution.py:28
  239.5 11.7 %cholesky.104 = f32[128,128]{1,0:T(8,128)S(1)} custom-call(f32[128,128]{1,0:T(8,128)S(1)} %cholesky.266), custom_call_target="Cholesky" | custom-call | tf_op jit(solution)/shard_map/jit(cholesky)/cholesky | solution.py:86
  251.4 9.8 %custom-call.32 = f32[1,128,128]{1,2,0:T(8,128)S(1)} custom-call(f32[1,128,128]{2,1,0:T(8,128)S(1)} %get-tuple-element.68), custom_call_target="InvertDiagBlocksLowerTriangular" | custom-call | tf_op jit(solution)/shard_map/jit(cholesky)/cholesky | solution.py:86
  261.9 12.1 %cholesky.217 = f32[128,128]{1,0:T(8,128)S(1)} custom-call(f32[128,128]{1,0:T(8,128)S(1)} %cholesky.270), custom_call_target="Cholesky" | custom-call | tf_op jit(solution)/shard_map/jit(cholesky)/cholesky | solution.py:86
  274.0 7.7 %all-to-all-start.5 = ((f32[32,32,1024]{2,1,0:T(8,128)}), f32[32,32,1024]{2,1,0:T(8,128)}, u32[]{:S(2)}, u32[]{:S(2)}) async-start(f32[32,32,1024]{2,1,0:T(8,128)} %bitcast.128), calls=%async_computation.5 | async-start | bytes 8388608 | tf_op jit(solution)/shard_map/all_to_all | solution.py:33
  281.7 9.8 %custom-call.33 = f32[1,128,128]{1,2,0:T(8,128)S(1)} custom-call(f32[1,128,128]{2,1,0:T(8,128)S(1)} %get-tuple-element.65), custom_call_target="InvertDiagBlocksLowerTriangular" | custom-call | tf_op jit(solution)/shard_map/jit(cholesky)/cholesky | solution.py:86
  292.2 11.7 %cholesky.238 = f32[128,128]{1,0:T(8,128)S(1)} custom-call(f32[128,128]{1,0:T(8,128)S(1)} %cholesky.275), custom_call_target="Cholesky" | custom-call | tf_op jit(solution)/shard_map/jit(cholesky)/cholesky | solution.py:86
  303.9 9.8 %custom-call.34 = f32[1,128,128]{1,2,0:T(8,128)S(1)} custom-call(f32[1,128,128]{2,1,0:T(8,128)S(1)} %get-tuple-element.62), custom_call_target="InvertDiagBlocksLowerTriangular" | custom-call | tf_op jit(solution)/shard_map/jit(cholesky)/cholesky | solution.py:86
  314.3 11.9 %cholesky.255 = f32[128,128]{1,0:T(8,128)S(1)} custom-call(f32[128,128]{1,0:T(8,128)S(1)} %convolution_subtract_fusion.6), custom_call_target="Cholesky" | custom-call | tf_op jit(solution)/shard_map/jit(cholesky)/cholesky | solution.py:86
  331.5 10.4 %while.1 = (s32[]{:T(128)}, f32[512,512]{1,0:T(8,128)S(1)}, s32[4,2]{0,1:T(2,128)S(1)}, f32[4,128,128]{2,1,0:T(8,128)}, s32[]{:T(128)}) while((s32[]{:T(128)}, f32[512,512]{1,0:T(8,128)S(1)}, s32[4,2]{0,1:T(2,128)S(1)}, f32[4,128,128]{2,1,0:T(8,128)}, s32[]{:T(128)}) %tuple.97), condition=%wide.while_cond, body=%wide.while_body.sunk | while | flops 2 | bytes 132705 | solution.py:92
  341.9 40.1 %custom-call.35 = f32[4,128,128]{1,2,0:T(8,128)S(1)} custom-call(f32[4,128,128]{2,1,0:T(8,128)} %get-tuple-element.21), custom_call_target="InvertDiagBlocksLowerTriangular" | custom-call | tf_op jit(solution)/shard_map/triangular_solve | solution.py:92
  382.7 2.9 fusion.84
  (104 shorter events, 46.3 us)
Async XLA Ops:
  7.2 109.7 %all-gather.3.cloned.1.call-start = ((), (), s32[]{:S(2)}) async-start(), calls=%async_computation.6 | async-start | bytes 7569408 | tf_op jit(solution)/shard_map/all_gather | solution.py:60
  9.0 203.3 %copy-start.4 = (pred[32]{0:T(512)(128)(4,1)}, pred[32]{0:T(512)(128)(4,1)S(1)}, u32[]{:S(2)}) copy-start(pred[32]{0:T(512)(128)(4,1)S(1)} %iota_compare_fusion.19) | copy-start | bytes 100
  12.9 11.8 %copy-start.6 = (s32[32]{0:T(128)S(1)}, s32[32]{0:T(128)}, u32[]{:S(2)}) copy-start(s32[32]{0:T(128)} %param.6) | copy-start | bytes 388
  12.9 62.5 %all-to-all-start = ((bf16[32,32,896]{2,0,1:T(8,128)(2,1)}), bf16[32,32,896]{2,0,1:T(8,128)(2,1)S(1)}, u32[]{:S(2)}, u32[]{:S(2)}) async-start(bf16[32,32,896]{2,0,1:T(8,128)(2,1)} %bitcast.127), calls=%async_computation | async-start | bytes 3670016 | tf_op jit(solution)/shard_map/all_to_all | solution.py:59
  75.4 91.9 %copy-start = (bf16[32,32,896]{2,0,1:T(8,128)(2,1)}, bf16[32,32,896]{2,0,1:T(8,128)(2,1)S(1)}, u32[]{:S(2)}) copy-start(bf16[32,32,896]{2,0,1:T(8,128)(2,1)S(1)} %all-to-all-done) | copy-start | bytes 5505028
  203.3 9.0 %copy-start.2 = (bf16[32,1024]{1,0:T(8,128)(2,1)S(1)}, bf16[32,1024]{1,0:T(8,128)(2,1)}, u32[]{:S(2)}) copy-start(bf16[32,1024]{1,0:T(8,128)(2,1)} %param.10) | copy-start | bytes 196612
  203.4 9.0 %copy-start.3 = (bf16[32,1024]{1,0:T(8,128)(2,1)S(1)}, bf16[32,1024]{1,0:T(8,128)(2,1)}, u32[]{:S(2)}) copy-start(bf16[32,1024]{1,0:T(8,128)(2,1)} %param.9) | copy-start | bytes 196612
  204.5 33.9 %all-to-all-start.4 = ((f32[32,16,512]{2,1,0:T(8,128)}), f32[32,16,512]{2,1,0:T(8,128)S(1)}, u32[]{:S(2)}, u32[]{:S(2)}) async-start(f32[32,16,512]{2,1,0:T(8,128)} %broadcast_in_dim.73), calls=%async_computation.4 | async-start | bytes 2097152 | tf_op jit(solution)/shard_map/all_to_all | solution.py:28
  212.1 119.0 %all-gather.5.cloned.1.call-start = ((), (), s32[]{:S(2)}) async-start(), calls=%async_computation.7 | async-start | bytes 2162688 | tf_op jit(solution)/shard_map/all_gather | solution.py:64
  274.0 123.9 %all-to-all-start.5 = ((f32[32,32,1024]{2,1,0:T(8,128)}), f32[32,32,1024]{2,1,0:T(8,128)}, u32[]{:S(2)}, u32[]{:S(2)}) async-start(f32[32,32,1024]{2,1,0:T(8,128)} %bitcast.128), calls=%async_computation.5 | async-start | bytes 8388608 | tf_op jit(solution)/shard_map/all_to_all | solution.py:33
  330.9 0.7 copy-start.9
  393.5 1.7 copy-start.1
  393.5 1.8 copy-start.7
  397.8 2.4 copy-start.5
  397.8 2.5 copy-start.8
Sparse Core Ops, SparseCore 0:
  11.6 105.2 all-gather.2
  216.1 81.9 all-gather.4
where the time goes:
time: 417 us; the launch traced here: 409 us
  other arithmetic  150 us (36%)
  waiting for transfers between devices  85.5 us (21%)
  blocking collectives  69.6 us (17%)
  matrix products  41.2 us (10%)
  starting transfers between devices  27.2 us (7%)
  local copies, waits for them, and re-layouts  18.3 us (4%)
  between operations  17.3 us (4%)
    another operation x14, other arithmetic, per_device(): factor = jnp.linalg.cholesky(system)  79 us
    all_gather x1, waiting for transfers between devices, per_device(): gathered = lax.all_gather(column_part, 'dp', axis=0, tiled=True)  41.5 us
    another operation x3, other arithmetic, per_device(): lax.linalg.triangular_solve(factor, middle, left_side=True, lower=True, t...  40.8 us
    all_to_all x1, blocking collectives, scatter_rows_sum(): lax.all_to_all(x.reshape((n, x.shape[0] // n) + x.shape[1:]), axis, 0, 0,...  33 us
    all_to_all x1, waiting for transfers between devices, per_device(): lax.all_to_all(masked_keys, 'dp', split_axis=1, concat_axis=0, tiled=True)  28.5 us
    all_to_all x1, blocking collectives, per_device(): lax.all_to_all(partial_q.astype(jnp.bfloat16).reshape((tensor_size, -1) +...  18.9 us
    all_to_all x1, blocking collectives, gather_rows(): lax.all_to_all(copies, axis, 0, 0, tiled=True)  17.7 us
    sub x1, other arithmetic, per_device(): row_of = owner * slot_count + compact - starts[owner]  15.8 us
  transfers between devices with their start and end apart: 5, of which 3 were waited for; matrix products, arithmetic and copies ran while one was open for 45% of the time, Pallas kernels for 0%

commit v1 on v0

--- a/solution.py
+++ b/solution.py
@@ -56,7 +56,9 @@
     own_compact = jnp.where(live_vec, starts[group_index] + slots, 0)
     masked_keys = jnp.where(live_slot, keys, jnp.zeros_like(keys))
     column_part = lax.dynamic_slice_in_dim(masked_keys, tensor_index * width_part, width_part, 1)
-    columns = lax.all_to_all(masked_keys, "dp", split_axis=1, concat_axis=0, tiled=True)
+    shards = jnp.split(masked_keys, lax.axis_size("dp"), axis=1)
+    incoming = lax.all_to_all(jnp.stack(shards), "dp", 0, 0)
+    columns = jnp.concatenate(incoming, axis=0)
     gathered = lax.all_gather(column_part, "dp", axis=0, tiled=True)
     change = (targets.astype(jnp.float32) - hidden.astype(jnp.float32)) / LAYERS_LEFT
     resid_local = jnp.where(live_slot, change, jnp.zeros_like(change)).astype(jnp.bfloat16)

time: 417 us -> 424 us (1.017)
  local copies, waits for them, and re-layouts: 18.3 us -> 37 us
  waiting for transfers between devices: 85.5 us -> 73.3 us
    unnamed x20 -> x51, local copies, waits for them, and re-layouts: 0.45 us -> 19.9 us
    all_gather x1, waiting for transfers between devices: 41.5 us -> 26 us  [per_device(): gathered = lax.all_gather(column_part, 'dp', axis=0, tiled=True)]
    another operation x13 -> x14, local copies, waits for them, and re-layouts: 10.5 us -> 11.1 us
  transfers between devices with their start and end apart: 5 -> 5, of which waited for: 3 -> 3; matrix products, arithmetic and copies ran while one was open for 45% -> 48% of each run, Pallas kernels for 0% -> 0%
where the time goes in v1:
time: 424 us; the launch traced here: 416 us
  other arithmetic  150 us (35%)
  waiting for transfers between devices  73.3 us (17%)
  blocking collectives  70 us (17%)
  matrix products  41.1 us (10%)
  local copies, waits for them, and re-layouts  37 us (9%)
  starting transfers between devices  27.2 us (6%)
  between operations  17.4 us (4%)
    another operation x14, other arithmetic, per_device(): factor = jnp.linalg.cholesky(system)  79 us
    another operation x3, other arithmetic, per_device(): lax.linalg.triangular_solve(factor, middle, left_side=True, lower=True, t...  40.8 us
    all_to_all x1, blocking collectives, scatter_rows_sum(): lax.all_to_all(x.reshape((n, x.shape[0] // n) + x.shape[1:]), axis, 0, 0,...  33.4 us
    all_to_all x1, waiting for transfers between devices, per_device(): incoming = lax.all_to_all(jnp.stack(shards), 'dp', 0, 0)  31.7 us
    all_gather x1, waiting for transfers between devices, per_device(): gathered = lax.all_gather(column_part, 'dp', axis=0, tiled=True)  26 us
    unnamed x51, local copies, waits for them, and re-layouts  19.9 us
    all_to_all x1, blocking collectives, per_device(): lax.all_to_all(partial_q.astype(jnp.bfloat16).reshape((tensor_size, -1) +...  19 us
    all_to_all x1, blocking collectives, gather_rows(): lax.all_to_all(copies, axis, 0, 0, tiled=True)  17.7 us
  transfers between devices with their start and end apart: 5, of which 3 were waited for; matrix products, arithmetic and copies ran while one was open for 48% of the time, Pallas kernels for 0%

profile of v1, /device:TPU:2, one launch (start us, length us, event | category | flops | bytes accessed | tf_op | source)
XLA Modules:
  0.0 415.5 jit_solution(13358900008816719965)
XLA Ops:
  31.5 11.8 %all-to-all-start = ((bf16[32,32,896]{2,1,0:T(8,128)(2,1)}), bf16[32,32,896]{2,1,0:T(8,128)(2,1)S(1)}, u32[]{:S(2)}, u32[]{:S(2)}) async-start(bf16[32,32,896]{2,1,0:T(8,128)(2,1)} %constant_dynamic-update-slice_fusion), calls=%async_computation | async-start | bytes 3670016 | tf_op jit(solution)/shard_map/all_to_all | solution.py:60
  45.1 4.4 %compare_select_fusion.1 = (s32[512,1]{0,1:T(1,128)S(1)}, s32[512,1]{0,1:T(1,128)S(1)}) fusion(s32[]{:T(128)} %bitcast.27, s32[]{:T(128)} %bitcast.28, s32[]{:T(128)} %bitcast.29, s32[]{:T(128)} %bitcast.30, s32[]{:T(128)} %bitcast.31, s32[]{:T(128)} %bitcast.33, s32[]{:T(128)} %bitcast.32, s32[512,1]{0,1:T(1,128)S(1)} %bitcast.256), kind=kLoop, calls=%fused_computation.199 | loop fusion | flops 7680 | bytes 6172 | tf_op jit(solution)/shard_map/gather | solution.py:49
  49.7 15.8 %select_subtract_fusion = s32[512]{0:T(512)S(1)} fusion(pred[512]{0:T(512)(128)(4,1)S(1)} %get-tuple-element.46, pred[512]{0:T(512)(128)(4,1)S(1)} %get-tuple-element.45, pred[512]{0:T(512)(128)(4,1)S(1)} %get-tuple-element.44, pred[512]{0:T(512)(128)(4,1)S(1)} %get-tuple-element.43, pred[512]{0:T(512)(128)(4,1)S(1)} %get-tuple-element.42, ...), kind=kLoop, calls=%fused_computation.208 | loop fusion | flops 14848 | bytes 19044 | tf_op jit(solution)/shard_map/sub | solution.py:49
  65.5 31.7 %all-to-all-done = bf16[32,32,896]{2,1,0:T(8,128)(2,1)S(1)} async-done(((bf16[32,32,896]{2,1,0:T(8,128)(2,1)}), bf16[32,32,896]{2,1,0:T(8,128)(2,1)S(1)}, u32[]{:S(2)}, u32[]{:S(2)}) %all-to-all-start) | async-done | bytes 1835040 | tf_op jit(solution)/shard_map/all_to_all | solution.py:60
  97.3 26.0 %all-gather.3.cloned.1.call-done = bf16[1024,3584]{1,0:T(8,128)(2,1)} async-done(((bf16[32,3584]{1,0:T(8,128)(2,1)}), bf16[1024,3584]{1,0:T(8,128)(2,1)}) %all-gather.3.cloned.1.call-update) | async-done | bytes 7340048 | tf_op jit(solution)/shard_map/all_gather | solution.py:62
  123.3 13.7 %convolution_convert_fusion.1 = bf16[512,896]{1,0:T(8,128)(2,1)} fusion(bf16[3584,896]{1,0:T(8,128)(2,1)} %param.8, bf16[1024,3584]{1,0:T(8,128)(2,1)} %all-gather.3.cloned.1.call-done, s32[512]{0:T(512)S(1)} %select_subtract_fusion), kind=kOutput, calls=%fused_computation.23 | convolution fusion | flops 7049248768 | bytes 14682112 | tf_op jit(solution)/shard_map/dot_general | solution.py:69
  137.0 19.0 %all_to_all.30 = bf16[8,64,896]{2,1,0:T(8,128)(2,1)S(1)} all-to-all(bf16[8,64,896]{2,1,0:T(8,128)(2,1)} %bitcast.254), channel_id=1, replica_groups=mesh['dp'=32,'tensor'=8] {'tensor'}, dimensions={0} | all-to-all | bytes 1835008 | tf_op jit(solution)/shard_map/all_to_all | solution.py:72
  156.2 17.7 %all_to_all.31 = bf16[8,64,896]{2,1,0:T(8,128)(2,1)} all-to-all(bf16[8,64,896]{2,1,0:T(8,128)(2,1)S(1)} %broadcast_in_dim.72), channel_id=1, replica_groups=mesh['dp'=32,'tensor'=8] {'tensor'}, dimensions={0} | all-to-all | bytes 1835008 | tf_op jit(solution)/shard_map/all_to_all | solution.py:28
  173.9 3.0 fusion.37
  176.9 33.4 %all_to_all.32 = f32[32,16,512]{2,1,0:T(8,128)S(1)} all-to-all(f32[32,16,512]{2,1,0:T(8,128)S(1)} %fusion.37), channel_id=1, replica_groups=mesh['dp'=32,'tensor'=8] {'dp'}, dimensions={0} | all-to-all | bytes 2097152 | tf_op jit(solution)/shard_map/all_to_all | solution.py:33
  211.5 7.5 %all-to-all-start.4 = ((f32[32,16,512]{2,1,0:T(8,128)}), f32[32,16,512]{2,1,0:T(8,128)S(1)}, u32[]{:S(2)}, u32[]{:S(2)}) async-start(f32[32,16,512]{2,1,0:T(8,128)} %broadcast_in_dim.73), calls=%async_computation.4 | async-start | bytes 2097152 | tf_op jit(solution)/shard_map/all_to_all | solution.py:28
  223.6 6.3 %fusion.88 = f32[1024,1024]{1,0:T(8,128)} fusion(bf16[1024,896]{1,0:T(8,128)(2,1)} %bitcast.251, bf16[1024,896]{1,0:T(8,128)(2,1)} %param.11), kind=kOutput, calls=%fused_computation.239 | convolution fusion | flops 1879048192 | bytes 7864320 | tf_op jit(solution)/shard_map/dot_general | solution.py:16
  229.9 15.5 %all-to-all-done.4 = f32[32,16,512]{2,1,0:T(8,128)S(1)} async-done(((f32[32,16,512]{2,1,0:T(8,128)}), f32[32,16,512]{2,1,0:T(8,128)S(1)}, u32[]{:S(2)}, u32[]{:S(2)}) %all-to-all-start.4) | async-done | bytes 1048608 | tf_op jit(solution)/shard_map/all_to_all | solution.py:28
  246.4 11.7 %cholesky.104 = f32[128,128]{1,0:T(8,128)S(1)} custom-call(f32[128,128]{1,0:T(8,128)S(1)} %cholesky.266), custom_call_target="Cholesky" | custom-call | tf_op jit(solution)/shard_map/jit(cholesky)/cholesky | solution.py:88
  258.3 9.8 %custom-call.32 = f32[1,128,128]{1,2,0:T(8,128)S(1)} custom-call(f32[1,128,128]{2,1,0:T(8,128)S(1)} %get-tuple-element.68), custom_call_target="InvertDiagBlocksLowerTriangular" | custom-call | tf_op jit(solution)/shard_map/jit(cholesky)/cholesky | solution.py:88
  268.8 12.1 %cholesky.217 = f32[128,128]{1,0:T(8,128)S(1)} custom-call(f32[128,128]{1,0:T(8,128)S(1)} %cholesky.270), custom_call_target="Cholesky" | custom-call | tf_op jit(solution)/shard_map/jit(cholesky)/cholesky | solution.py:88
  280.9 7.6 %all-to-all-start.5 = ((f32[32,32,1024]{2,1,0:T(8,128)}), f32[32,32,1024]{2,1,0:T(8,128)}, u32[]{:S(2)}, u32[]{:S(2)}) async-start(f32[32,32,1024]{2,1,0:T(8,128)} %bitcast.248), calls=%async_computation.5 | async-start | bytes 8388608 | tf_op jit(solution)/shard_map/all_to_all | solution.py:33
  288.6 9.8 %custom-call.33 = f32[1,128,128]{1,2,0:T(8,128)S(1)} custom-call(f32[1,128,128]{2,1,0:T(8,128)S(1)} %get-tuple-element.65), custom_call_target="InvertDiagBlocksLowerTriangular" | custom-call | tf_op jit(solution)/shard_map/jit(cholesky)/cholesky | solution.py:88
  299.1 11.7 %cholesky.238 = f32[128,128]{1,0:T(8,128)S(1)} custom-call(f32[128,128]{1,0:T(8,128)S(1)} %cholesky.275), custom_call_target="Cholesky" | custom-call | tf_op jit(solution)/shard_map/jit(cholesky)/cholesky | solution.py:88
  310.8 9.8 %custom-call.34 = f32[1,128,128]{1,2,0:T(8,128)S(1)} custom-call(f32[1,128,128]{2,1,0:T(8,128)S(1)} %get-tuple-element.62), custom_call_target="InvertDiagBlocksLowerTriangular" | custom-call | tf_op jit(solution)/shard_map/jit(cholesky)/cholesky | solution.py:88
  321.2 11.9 %cholesky.255 = f32[128,128]{1,0:T(8,128)S(1)} custom-call(f32[128,128]{1,0:T(8,128)S(1)} %convolution_subtract_fusion.6), custom_call_target="Cholesky" | custom-call | tf_op jit(solution)/shard_map/jit(cholesky)/cholesky | solution.py:88
  338.4 10.4 %while.1 = (s32[]{:T(128)}, f32[512,512]{1,0:T(8,128)S(1)}, s32[4,2]{0,1:T(2,128)S(1)}, f32[4,128,128]{2,1,0:T(8,128)}, s32[]{:T(128)}) while((s32[]{:T(128)}, f32[512,512]{1,0:T(8,128)S(1)}, s32[4,2]{0,1:T(2,128)S(1)}, f32[4,128,128]{2,1,0:T(8,128)}, s32[]{:T(128)}) %tuple.97), condition=%wide.while_cond, body=%wide.while_body.sunk | while | flops 2 | bytes 132205 | solution.py:94
  348.8 40.1 %custom-call.35 = f32[4,128,128]{1,2,0:T(8,128)S(1)} custom-call(f32[4,128,128]{2,1,0:T(8,128)} %get-tuple-element.21), custom_call_target="InvertDiagBlocksLowerTriangular" | custom-call | tf_op jit(solution)/shard_map/triangular_solve | solution.py:94
  389.6 2.9 fusion.84
  (135 shorter events, 64.9 us)
Async XLA Ops:
  7.2 116.2 %all-gather.3.cloned.1.call-start = ((), (), s32[]{:S(2)}) async-start(), calls=%async_computation.6 | async-start | bytes 7569408 | tf_op jit(solution)/shard_map/all_gather | solution.py:62
  9.0 210.2 %copy-start.4 = (pred[32]{0:T(512)(128)(4,1)}, pred[32]{0:T(512)(128)(4,1)S(1)}, u32[]{:S(2)}) copy-start(pred[32]{0:T(512)(128)(4,1)S(1)} %iota_compare_fusion.19) | copy-start | bytes 100
  31.5 11.8 %copy-start.6 = (s32[32]{0:T(128)S(1)}, s32[32]{0:T(128)}, u32[]{:S(2)}) copy-start(s32[32]{0:T(128)} %param.6) | copy-start | bytes 388
  31.5 65.7 %all-to-all-start = ((bf16[32,32,896]{2,1,0:T(8,128)(2,1)}), bf16[32,32,896]{2,1,0:T(8,128)(2,1)S(1)}, u32[]{:S(2)}, u32[]{:S(2)}) async-start(bf16[32,32,896]{2,1,0:T(8,128)(2,1)} %constant_dynamic-update-slice_fusion), calls=%async_computation | async-start | bytes 3670016 | tf_op jit(solution)/shard_map/all_to_all | solution.py:60
  97.3 76.6 %copy-start = (bf16[32,32,896]{2,1,0:T(8,128)(2,1)}, bf16[32,32,896]{2,1,0:T(8,128)(2,1)S(1)}, u32[]{:S(2)}) copy-start(bf16[32,32,896]{2,1,0:T(8,128)(2,1)S(1)} %all-to-all-done) | copy-start | bytes 5505028
  210.3 8.9 %copy-start.2 = (bf16[32,1024]{1,0:T(8,128)(2,1)S(1)}, bf16[32,1024]{1,0:T(8,128)(2,1)}, u32[]{:S(2)}) copy-start(bf16[32,1024]{1,0:T(8,128)(2,1)} %param.10) | copy-start | bytes 196612
  210.3 8.9 %copy-start.3 = (bf16[32,1024]{1,0:T(8,128)(2,1)S(1)}, bf16[32,1024]{1,0:T(8,128)(2,1)}, u32[]{:S(2)}) copy-start(bf16[32,1024]{1,0:T(8,128)(2,1)} %param.9) | copy-start | bytes 196612
  211.5 33.9 %all-to-all-start.4 = ((f32[32,16,512]{2,1,0:T(8,128)}), f32[32,16,512]{2,1,0:T(8,128)S(1)}, u32[]{:S(2)}, u32[]{:S(2)}) async-start(f32[32,16,512]{2,1,0:T(8,128)} %broadcast_in_dim.73), calls=%async_computation.4 | async-start | bytes 2097152 | tf_op jit(solution)/shard_map/all_to_all | solution.py:28
  219.0 118.9 %all-gather.5.cloned.1.call-start = ((), (), s32[]{:S(2)}) async-start(), calls=%async_computation.7 | async-start | bytes 2162688 | tf_op jit(solution)/shard_map/all_gather | solution.py:66
  280.9 123.8 %all-to-all-start.5 = ((f32[32,32,1024]{2,1,0:T(8,128)}), f32[32,32,1024]{2,1,0:T(8,128)}, u32[]{:S(2)}, u32[]{:S(2)}) async-start(f32[32,32,1024]{2,1,0:T(8,128)} %bitcast.248), calls=%async_computation.5 | async-start | bytes 8388608 | tf_op jit(solution)/shard_map/all_to_all | solution.py:33
  337.8 0.7 copy-start.9
  400.4 1.7 copy-start.1
  400.4 1.8 copy-start.7
  404.7 2.4 copy-start.5
  404.7 2.5 copy-start.8
Sparse Core Ops, SparseCore 0:
  11.6 111.6 all-gather.2
  223.0 82.1 all-gather.4
